TPU v7x, 32 devices: a whole 2x2x4 slice. The times are simulated.
32 devices in a mesh: seq: 8 (over y, x, core), head: 4 (over z).
Axes of the slice: x: 2, y: 2, z: 4, core: 2. Of those that a mesh axis runs over, the one named last changes fastest.
Arguments:
- query_rows: bfloat16 [1024, 2304], P(('seq', 'head')), may hold values from -6 to 6
- key_rows: bfloat16 [1024, 2304], P(('seq', 'head')), may hold values from -6 to 6
- value_rows: bfloat16 [1024, 2304], P(('seq', 'head')), may hold values from -6 to 6
- residual_in: bfloat16 [1024, 2304], P(('seq', 'head')), may hold values from -40 to 40
- norm_gain: float32 [2304], replicated, may hold values from 0.1 to 1.9
- router_weight: bfloat16 [2304, 8], replicated, may hold values from -0.125 to 0.125
- segment_ids: int32 [1024], P('seq'), may hold values from 0 to 3, never falling along the last dimension, each value on 1 to 897 neighbouring positions
- expert_ids: int32 [1024, 2], P(('seq', 'head')), may hold values from 0 to 7, all different within a row; in each aligned block of 32 rows (0 to 31, 32 to 63, ...) at most 9 rows name the same one
- gate_weight: bfloat16 [2304, 23040], P(None, ('seq', 'head')), may hold values from -0.125 to 0.125
- up_weight: bfloat16 [2304, 23040], P(None, ('seq', 'head')), may hold values from -0.125 to 0.125
- down_weight: bfloat16 [2304, 23040], P(None, ('seq', 'head')), may hold values from -0.109375 to 0.109375
- out_weight: bfloat16 [2304, 2304], P('head'), may hold values from -0.125 to 0.125
Outputs:
- residual_out: bfloat16 [1024, 2304], P(('seq', 'head'))
- key_cache: bfloat16 [1024, 2304], P('seq', 'head')
- value_cache: bfloat16 [1024, 2304], P('seq', 'head')
Inputs may be any that keep to these rules, and one draw needn't show every extreme that they name: `segment_ids`: each segment covers at most 897 tokens. `expert_ids`: in the rows of one device no expert is named more than 9 times.
All inputs are finite; a program needn't handle non-finite values.
Results may differ from a plain program's by a relative error of at most 0.005.
Values may be sent and summed in bfloat16 or wider, within the bound.
No kernel may reach another device: no remote copies, remote signals or barrier semaphores. Data moves between devices by JAX's collectives and lax.ppermute only.
A program may use at most 128 MiB of HBM per device.

v0:
```python
import math
import jax
import jax.numpy as jnp
from jax import lax
from jax.sharding import PartitionSpec as P

D = 2304
HDIM = 64
LEVELS = 4
CAP = 9
residual_scale = 1.4 / math.sqrt(40.0)
norm_epsilon = 1e-05


def passed_along(value, axis, by):
    length = lax.axis_size(axis)
    pairs = [(i, i + by) for i in range(length) if 0 <= i + by < length]
    return lax.ppermute(value, axis, pairs)


def score_piece(queries, key_piece, piece_allowed):
    raw_scores = jnp.einsum(
        "qhd,khd->hqk", queries, key_piece, preferred_element_type=jnp.float32
    ) * queries.shape[2] ** (-0.5)
    return jnp.where(piece_allowed[None], raw_scores, -jnp.inf)


def mix_piece(rounded_piece, value_piece):
    return jnp.einsum(
        "hqk,khd->qhd", rounded_piece, value_piece, preferred_element_type=jnp.float32
    )


def per_device(
    query_rows,
    key_rows,
    value_rows,
    residual_in,
    norm_gain,
    router_weight,
    segment_ids,
    expert_ids,
    gate_weight,
    up_weight,
    down_weight,
    out_weight,
):
    head_count = lax.axis_size("head")
    seq_count = lax.axis_size("seq")
    tok_local = query_rows.shape[0]
    group_width = query_rows.shape[1] // head_count
    heads_here = group_width // HDIM
    stretch_len = tok_local * head_count
    span_count = min(2**LEVELS * 32 // tok_local, seq_count)
    gate_full, up_full, down_full = (
        lax.all_gather(gate_weight, "head", axis=1, tiled=True),
        lax.all_gather(up_weight, "head", axis=1, tiled=True),
        lax.all_gather(down_weight, "head", axis=1, tiled=True),
    )
    expert_count = router_weight.shape[1]
    replicas = seq_count // expert_count
    seq_place = lax.axis_index("seq")
    query_head, key_head, value_head = (
        lax.all_to_all(
            query_rows.reshape(tok_local, head_count, group_width),
            "head",
            split_axis=1,
            concat_axis=0,
            tiled=True,
        ),
        lax.all_to_all(
            key_rows.reshape(tok_local, head_count, group_width),
            "head",
            split_axis=1,
            concat_axis=0,
            tiled=True,
        ),
        lax.all_to_all(
            value_rows.reshape(tok_local, head_count, group_width),
            "head",
            split_axis=1,
            concat_axis=0,
            tiled=True,
        ),
    )
    query_head = query_head.reshape(stretch_len, group_width)
    key_head = key_head.reshape(stretch_len, group_width)
    value_head = value_head.reshape(stretch_len, group_width)
    front_rows = (span_count - 1) * stretch_len
    key_window = jnp.concatenate((jnp.zeros((front_rows, group_width), jnp.bfloat16), key_head), 0)
    value_window = jnp.concatenate(
        (jnp.zeros((front_rows, group_width), jnp.bfloat16), value_head), 0
    )
    segment_window = jnp.concatenate((jnp.zeros((front_rows,), jnp.int32), segment_ids), 0)

    def advance(step_index, carried):
        moving, keys_held, values_held, segments_held = carried
        moving = passed_along((moving[0], moving[1], moving[2]), "seq", 1)
        write_place = (span_count - 1 - step_index) * stretch_len
        keys_held = lax.dynamic_update_slice_in_dim(keys_held, moving[0], write_place, 0)
        values_held = lax.dynamic_update_slice_in_dim(values_held, moving[1], write_place, 0)
        segments_held = lax.dynamic_update_slice_in_dim(segments_held, moving[2], write_place, 0)
        return (moving, keys_held, values_held, segments_held)

    moving_final, key_window, value_window, segment_window = lax.fori_loop(
        1,
        span_count,
        advance,
        ((key_head, value_head, segment_ids), key_window, value_window, segment_window),
    )
    key_total = span_count * stretch_len
    query_place = seq_place * stretch_len + jnp.arange(stretch_len, dtype=jnp.int32)
    key_place = (seq_place - span_count + 1) * stretch_len + jnp.arange(key_total, dtype=jnp.int32)
    allowed = (
        (segment_window[None, :] == segment_ids[:, None])
        & (key_place[None, :] <= query_place[:, None])
        & (key_place[None, :] >= 0)
    )
    queries = query_head.reshape(stretch_len, heads_here, HDIM)
    keys_all = key_window.reshape(key_total, heads_here, HDIM)
    values_all = value_window.reshape(key_total, heads_here, HDIM)
    masked = score_piece(queries, keys_all, allowed)
    row_max = jnp.max(masked, -1, keepdims=True)
    weights = jnp.where(allowed[None], jnp.exp(masked - row_max), 0.0)
    totals = jnp.sum(weights, -1)
    mixture = mix_piece(weights.astype(jnp.bfloat16), values_all)
    attention = (
        (mixture / jnp.transpose(totals)[:, :, None])
        .astype(jnp.bfloat16)
        .reshape(stretch_len, group_width)
    )
    attended_sum = lax.psum_scatter(
        jnp.dot(attention, out_weight, preferred_element_type=jnp.float32).astype(jnp.bfloat16),
        "head",
        scatter_dimension=0,
        tiled=True,
    ).astype(jnp.float32)
    middle = (residual_in.astype(jnp.float32) + residual_scale * attended_sum).astype(jnp.bfloat16)
    middle_wide = middle.astype(jnp.float32)
    mean_square = jnp.mean(middle_wide * middle_wide, -1, keepdims=True)
    normed = (middle_wide * lax.rsqrt(mean_square + norm_epsilon) * norm_gain).astype(jnp.bfloat16)
    route_count = expert_ids.shape[1]
    logits = jnp.dot(normed, router_weight, preferred_element_type=jnp.float32)
    route_hot = expert_ids[:, :, None] == jnp.arange(expert_count, dtype=jnp.int32)[None, None, :]
    chosen = jnp.sum(jnp.where(route_hot, logits[:, None, :], 0.0), -1)
    first_weight = 1.0 / (1.0 + jnp.exp(chosen[:, 1] - chosen[:, 0]))
    second_weight = 1.0 / (1.0 + jnp.exp(chosen[:, 0] - chosen[:, 1]))
    flat_hot = route_hot.reshape(tok_local * route_count, expert_count).astype(jnp.int32)
    before_count = jnp.cumsum(flat_hot, 0) - flat_hot
    route_rank = jnp.sum(before_count * flat_hot, -1)
    slot_ids = (expert_ids.reshape(-1) * CAP + route_rank).reshape(tok_local, route_count)
    slot_total = expert_count * CAP
    dispatch = jnp.any(
        slot_ids[None, :, :] == jnp.arange(slot_total, dtype=jnp.int32)[:, None, None], -1
    ).astype(jnp.bfloat16)
    packed = (
        jnp.dot(dispatch, normed, preferred_element_type=jnp.float32)
        .astype(jnp.bfloat16)
        .reshape(expert_count, CAP, D)
    )
    outgoing = jnp.broadcast_to(packed[:, None], (expert_count, replicas, CAP, D)).reshape(
        seq_count, CAP, D
    )
    arrived = lax.all_to_all(outgoing, "seq", split_axis=0, concat_axis=0, tiled=True)
    slot_count = arrived.shape[1]
    flat_rows = arrived.reshape(seq_count * slot_count, D)
    gate_act = jnp.dot(flat_rows, gate_full, preferred_element_type=jnp.float32)
    up_act = jnp.dot(flat_rows, up_full, preferred_element_type=jnp.float32)
    hidden = (jax.nn.silu(gate_act) * up_act).astype(jnp.bfloat16)
    shard_out = lax.dot_general(
        hidden, down_full, (((1,), (1,)), ((), ())), preferred_element_type=jnp.float32
    ).astype(jnp.bfloat16)
    returned = lax.all_to_all(
        shard_out.reshape(seq_count, slot_count, D), "seq", split_axis=0, concat_axis=0, tiled=True
    )
    expert_out = jnp.sum(
        returned.reshape(expert_count, replicas, CAP, D).astype(jnp.float32), 1
    ).reshape(slot_total, D)
    first_rows = expert_out[slot_ids[:, 0]]
    second_rows = expert_out[slot_ids[:, 1]]
    moe_sum = first_weight[:, None] * first_rows + second_weight[:, None] * second_rows
    residual_out = (middle_wide + residual_scale * moe_sum).astype(jnp.bfloat16)
    return (residual_out, key_head, value_head)


def solution(mesh):
    return jax.shard_map(
        per_device,
        mesh=mesh,
        in_specs=(
            P(("seq", "head"), None),
            P(("seq", "head"), None),
            P(("seq", "head"), None),
            P(("seq", "head"), None),
            P(),
            P(),
            P("seq"),
            P(("seq", "head"), None),
            P(None, ("seq", "head")),
            P(None, ("seq", "head")),
            P(None, ("seq", "head")),
            P("head", None),
        ),
        out_specs=(P(("seq", "head"), None), P("seq", "head"), P("seq", "head")),
        check_vma=False,
    )
```

profile of v0, /device:TPU:0, one launch (start us, length us, event | category | flops | bytes accessed | tf_op | source)
XLA Modules:
  0.0 894.4 jit_solution(14546956432762249407)
XLA Ops:
  9.1 6.3 all-to-all-start
  21.9 3.3 all-to-all-start.1
  27.1 4.1 all-to-all-done.1
  36.5 88.6 %while.23 = (s32[]{:T(128)}, bf16[128,576]{1,0:T(8,128)(2,1)}, bf16[128,576]{1,0:T(8,128)(2,1)}, s32[128]{0:T(128)S(1)}, bf16[1024,576]{1,0:T(8,128)(2,1)}, /*in...) while((s32[]{:T(128)}, bf16[128,576]{1,0:T(8,128)(2,1)}, ...), condition=%wide.region_1.0_spmd, body=%wide.region_0.0_spmd.sunk | while | flops 7 | bytes 2396467 | solution.py:105
  37.8 4.1 collective-permute-start.1
  47.5 3.4 collective-permute-start
  50.9 4.2 collective-permute-start.1
  60.6 4.3 collective-permute-start
  64.9 4.2 collective-permute-start.1
  77.5 4.2 collective-permute-start.1
  90.1 4.2 collective-permute-start.1
  102.7 4.2 collective-permute-start.1
  115.3 4.2 collective-permute-start.1
  131.8 5.3 fusion.41
  144.2 21.1 %reduce-scatter.2.cloned.1.call-done = bf16[32,2304]{1,0:T(8,128)(2,1)} async-done(((bf16[128,2304]{1,0:T(8,128)(2,1)}), bf16[32,2304]{1,0:T(8,128)(2,1)}) %reduce-scatter.2.cloned.1.call-update) | async-done | bytes 147472 | tf_op jit(solution)/shard_map/reduce_scatter | solution.py:132
  167.7 3.8 all-to-all-start.3
  173.3 8.6 all-to-all-done.3
  182.1 212.7 %all-gather.4.cloned.1.call-done = bf16[2304,2880]{0,1:T(8,128)(2,1)} async-done(((bf16[2304,720]{0,1:T(8,128)(2,1)}), bf16[2304,2880]{0,1:T(8,128)(2,1)}) %all-gather.4.cloned.1.call-update) | async-done | bytes 13271056 | tf_op jit(solution)/shard_map/all_gather | solution.py:56
  394.8 8.8 fusion.46
  403.7 220.4 %all-gather.6.cloned.1.call-done = bf16[2304,2880]{0,1:T(8,128)(2,1)} async-done(((bf16[2304,720]{0,1:T(8,128)(2,1)}), bf16[2304,2880]{0,1:T(8,128)(2,1)}) %all-gather.6.cloned.1.call-update) | async-done | bytes 13271056 | tf_op jit(solution)/shard_map/all_gather | solution.py:57
  624.1 229.1 %all-gather.8.cloned.1.call-done = bf16[2304,2880]{0,1:T(8,128)(2,1)} async-done(((bf16[2304,720]{0,1:T(8,128)(2,1)}), bf16[2304,2880]{0,1:T(8,128)(2,1)}) %all-gather.8.cloned.1.call-update) | async-done | bytes 13271056 | tf_op jit(solution)/shard_map/all_gather | solution.py:58
  853.2 14.9 %convolution_convert_fusion.1 = bf16[72,2304]{1,0:T(8,128)(2,1)S(1)} fusion(bf16[2304,2880]{0,1:T(8,128)(2,1)} %all-gather.8.cloned.1.call-done, bf16[72,2304]{1,0:T(8,128)(2,1)S(1)} %reshape.164, bf16[2304,2880]{0,1:T(8,128)(2,1)} %all-gather.6.cloned.1.call-done, f32[72,2880]{1,0:T(8,128)S(1)} %fusion.46), kind=kOutput, calls=%fused_computation.11 | convolution fusion | flops 1912439808 | bytes 28035072 | tf_op jit(solution)/shard_map/dot_general | solution.py:170
  869.0 3.7 all-to-all-start.4
  872.7 10.4 %all-to-all-done.4 = bf16[8,9,2304]{2,1,0:T(8,128)(2,1)S(1)} async-done(((bf16[8,9,2304]{2,1,0:T(8,128)(2,1)}), bf16[8,9,2304]{2,1,0:T(8,128)(2,1)S(1)}, u32[]{:S(2)}, u32[]{:S(2)}) %all-to-all-start.4) | async-done | bytes 331808 | tf_op jit(solution)/shard_map/all_to_all | solution.py:173
  (148 shorter events, 90.9 us)
Async XLA Ops:
  9.1 12.7 %all-to-all-start = ((bf16[32,4,576]{2,0,1:T(8,128)(2,1)}), bf16[32,4,576]{2,0,1:T(8,128)(2,1)S(1)}, u32[]{:S(2)}, u32[]{:S(2)}) async-start(bf16[32,4,576]{2,0,1:T(8,128)(2,1)} %copy.57), calls=%async_computation | async-start | bytes 327680 | tf_op jit(solution)/shard_map/all_to_all | solution.py:71
  21.9 9.3 %all-to-all-start.1 = ((bf16[32,4,576]{2,0,1:T(8,128)(2,1)}), bf16[32,4,576]{2,0,1:T(8,128)(2,1)S(1)}, u32[]{:S(2)}, u32[]{:S(2)}) async-start(bf16[32,4,576]{2,0,1:T(8,128)(2,1)} %copy.58), calls=%async_computation.1 | async-start | bytes 327680 | tf_op jit(solution)/shard_map/all_to_all | solution.py:78
  31.2 96.2 %all-to-all-start.2 = ((bf16[32,4,576]{2,0,1:T(8,128)(2,1)}), bf16[32,4,576]{2,0,1:T(8,128)(2,1)S(1)}, u32[]{:S(2)}, u32[]{:S(2)}) async-start(bf16[32,4,576]{2,0,1:T(8,128)(2,1)} %copy.61), calls=%async_computation.2 | async-start | bytes 327680 | tf_op jit(solution)/shard_map/all_to_all | solution.py:64
  34.6 130.7 %reduce-scatter.2.cloned.1.call-start = ((), (), s32[]{:S(2)}) async-start(), calls=%async_computation.6 | async-start | bytes 737280 | tf_op jit(solution)/shard_map/reduce_scatter | solution.py:132
  36.5 8.3 collective-permute-start
  37.8 8.4 collective-permute-start.1
  41.9 2.7 collective-permute-start.2
  47.5 10.5 %collective-permute-start = (bf16[128,576]{1,0:T(8,128)(2,1)}, bf16[128,576]{1,0:T(8,128)(2,1)S(1)}, u32[]{:S(2)}, u32[]{:S(2)}) collective-permute-start(bf16[128,576]{1,0:T(8,128)(2,1)} %get-tuple-element.230), channel_id=1, source_target_pairs={{0,4},{4,8},{8,12},{12,16},{16,20},{20,24},{24,28},{1,5},{5,9},{9,... | collective-permute-start | bytes 442376 | tf_op jit(solution)/shard_map/while/body/eval_jaxpr/ppermute | solution.py:18
  50.9 8.4 collective-permute-start.1
  60.6 11.4 %collective-permute-start = (bf16[128,576]{1,0:T(8,128)(2,1)}, bf16[128,576]{1,0:T(8,128)(2,1)S(1)}, u32[]{:S(2)}, u32[]{:S(2)}) collective-permute-start(bf16[128,576]{1,0:T(8,128)(2,1)} %get-tuple-element.230), channel_id=1, source_target_pairs={{0,4},{4,8},{8,12},{12,16},{16,20},{20,24},{24,28},{1,5},{5,9},{9,... | collective-permute-start | bytes 442376 | tf_op jit(solution)/shard_map/while/body/eval_jaxpr/ppermute | solution.py:18
  64.9 8.4 collective-permute-start.1
  74.7 9.9 %collective-permute-start = (bf16[128,576]{1,0:T(8,128)(2,1)}, bf16[128,576]{1,0:T(8,128)(2,1)S(1)}, u32[]{:S(2)}, u32[]{:S(2)}) collective-permute-start(bf16[128,576]{1,0:T(8,128)(2,1)} %get-tuple-element.230), channel_id=1, source_target_pairs={{0,4},{4,8},{8,12},{12,16},{16,20},{20,24},{24,28},{1,5},{5,9},{9,... | collective-permute-start | bytes 442376 | tf_op jit(solution)/shard_map/while/body/eval_jaxpr/ppermute | solution.py:18
  77.5 8.4 collective-permute-start.1
  87.3 9.9 %collective-permute-start = (bf16[128,576]{1,0:T(8,128)(2,1)}, bf16[128,576]{1,0:T(8,128)(2,1)S(1)}, u32[]{:S(2)}, u32[]{:S(2)}) collective-permute-start(bf16[128,576]{1,0:T(8,128)(2,1)} %get-tuple-element.230), channel_id=1, source_target_pairs={{0,4},{4,8},{8,12},{12,16},{16,20},{20,24},{24,28},{1,5},{5,9},{9,... | collective-permute-start | bytes 442376 | tf_op jit(solution)/shard_map/while/body/eval_jaxpr/ppermute | solution.py:18
  90.1 8.4 collective-permute-start.1
  99.8 9.9 %collective-permute-start = (bf16[128,576]{1,0:T(8,128)(2,1)}, bf16[128,576]{1,0:T(8,128)(2,1)S(1)}, u32[]{:S(2)}, u32[]{:S(2)}) collective-permute-start(bf16[128,576]{1,0:T(8,128)(2,1)} %get-tuple-element.230), channel_id=1, source_target_pairs={{0,4},{4,8},{8,12},{12,16},{16,20},{20,24},{24,28},{1,5},{5,9},{9,... | collective-permute-start | bytes 442376 | tf_op jit(solution)/shard_map/while/body/eval_jaxpr/ppermute | solution.py:18
  102.7 8.4 collective-permute-start.1
  112.5 9.9 %collective-permute-start = (bf16[128,576]{1,0:T(8,128)(2,1)}, bf16[128,576]{1,0:T(8,128)(2,1)S(1)}, u32[]{:S(2)}, u32[]{:S(2)}) collective-permute-start(bf16[128,576]{1,0:T(8,128)(2,1)} %get-tuple-element.230), channel_id=1, source_target_pairs={{0,4},{4,8},{8,12},{12,16},{16,20},{20,24},{24,28},{1,5},{5,9},{9,... | collective-permute-start | bytes 442376 | tf_op jit(solution)/shard_map/while/body/eval_jaxpr/ppermute | solution.py:18
  115.3 8.4 collective-permute-start.1
  141.2 253.6 %all-gather.4.cloned.1.call-start = ((), (), s32[]{:S(2)}) async-start(), calls=%async_computation.7 | async-start | bytes 16588800 | tf_op jit(solution)/shard_map/all_gather | solution.py:56
  142.0 482.1 %all-gather.6.cloned.1.call-start = ((), (), s32[]{:S(2)}) async-start(), calls=%async_computation.8 | async-start | bytes 16588800 | tf_op jit(solution)/shard_map/all_gather | solution.py:57
  142.7 710.4 %all-gather.8.cloned.1.call-start = ((), (), s32[]{:S(2)}) async-start(), calls=%async_computation.9 | async-start | bytes 16588800 | tf_op jit(solution)/shard_map/all_gather | solution.py:58
  167.7 14.2 %all-to-all-start.3 = ((bf16[8,9,2304]{2,1,0:T(8,128)(2,1)}), bf16[8,9,2304]{2,1,0:T(8,128)(2,1)S(1)}, u32[]{:S(2)}, u32[]{:S(2)}) async-start(bf16[8,9,2304]{2,1,0:T(8,128)(2,1)} %reshape_broadcast_in_dim_reshape.3), calls=%async_computation.4 | async-start | bytes 1179648 | tf_op jit(solution)/shard_map/all_to_all | solution.py:164
  869.0 14.1 %all-to-all-start.4 = ((bf16[8,9,2304]{2,1,0:T(8,128)(2,1)}), bf16[8,9,2304]{2,1,0:T(8,128)(2,1)S(1)}, u32[]{:S(2)}, u32[]{:S(2)}) async-start(bf16[8,9,2304]{2,1,0:T(8,128)(2,1)} %reshape.165), calls=%async_computation.5 | async-start | bytes 1179648 | tf_op jit(solution)/shard_map/all_to_all | solution.py:173
  (14 other events, 256.6 us)
Sparse Core Ops, SparseCore 0:
  141.3 23.9 reduce-scatter.1
  166.9 227.8 all-gather.3
  396.4 227.6 all-gather.5
  625.5 227.6 all-gather.7
where the time goes:
time: 896 us; the launch traced here: 894 us
  waiting for transfers between devices  716 us (80%)
  starting transfers between devices  83.3 us (9%)
  local copies, waits for them, and re-layouts  42.8 us (5%)
  matrix products  33.7 us (4%)
  between operations  14 us (2%)
    all_gather x1, waiting for transfers between devices, per_device(): lax.all_gather(down_weight, 'head', axis=1, tiled=True)  229 us
    all_gather x1, waiting for transfers between devices, per_device(): lax.all_gather(up_weight, 'head', axis=1, tiled=True)  220 us
    all_gather x1, waiting for transfers between devices, per_device(): lax.all_gather(gate_weight, 'head', axis=1, tiled=True)  213 us
    ppermute x21, starting transfers between devices, passed_along(): return lax.ppermute(value, axis, pairs)  62.7 us
    reduce_scatter x1, waiting for transfers between devices, per_device(): lax.psum_scatter(jnp.dot(attention, out_weight, preferred_element_type=jn...  21.1 us
  transfers between devices with their start and end apart: 30, of which 15 were waited for; matrix products, arithmetic and copies ran while one was open for 5% of the time, Pallas kernels for 0%

commit v1 on v0

--- a/solution.py
+++ b/solution.py
@@ -10,6 +10,19 @@
 CAP = 9
 residual_scale = 1.4 / math.sqrt(40.0)
 norm_epsilon = 1e-05
+
+
+def collect(x, axis, dim):
+    ways = lax.axis_size(axis)
+    up = [(d, (d + 1) % ways) for d in range(ways)]
+    down = [(d, (d - 1) % ways) for d in range(ways)]
+    earlier, later = ([x], [x])
+    for _ in range(ways // 2):
+        earlier.append(lax.ppermute(earlier[-1], axis, up))
+    for _ in range((ways - 1) // 2):
+        later.append(lax.ppermute(later[-1], axis, down))
+    line = jnp.concatenate([*earlier[::-1], *later[1:]], axis=dim)
+    return jnp.roll(line, (lax.axis_index(axis) - ways // 2) * x.shape[dim], axis=dim)
 
 
 def passed_along(value, axis, by):
@@ -53,7 +66,7 @@
     stretch_len = tok_local * head_count
     span_count = min(2**LEVELS * 32 // tok_local, seq_count)
     gate_full, up_full, down_full = (
-        lax.all_gather(gate_weight, "head", axis=1, tiled=True),
+        collect(gate_weight, "head", 1),
         lax.all_gather(up_weight, "head", axis=1, tiled=True),
         lax.all_gather(down_weight, "head", axis=1, tiled=True),
     )

time: 896 us -> 855 us (0.954)
  waiting for transfers between devices: 716 us -> 596 us
  starting transfers between devices: 83.3 us -> 132 us
  local copies, waits for them, and re-layouts: 42.8 us -> 72.3 us
    ppermute x0 -> x3, waiting for transfers between devices: none -> 366 us  [the longest x2 248 us: collect(): earlier.append(lax.ppermute(earlier[-1], axis, up))]
    all_gather x1, waiting for transfers between devices: 220 us -> 0.01 us  [per_device(): lax.all_gather(up_weight, 'head', axis=1, tiled=True)]
    all_gather x1 -> x0, waiting for transfers between devices: 213 us -> none  [per_device(): lax.all_gather(gate_weight, 'head', axis=1, tiled=True)]
    ppermute x0 -> x3, starting transfers between devices: none -> 46.3 us  [the longest x2 46.3 us: collect(): earlier.append(lax.ppermute(earlier[-1], axis, up))]
    all_gather x1, waiting for transfers between devices: 229 us -> 198 us  [per_device(): lax.all_gather(down_weight, 'head', axis=1, tiled=True)]
    unnamed x21 -> x30, local copies, waits for them, and re-layouts: 3.05 us -> 27.3 us
    reduce_scatter x1, waiting for transfers between devices: 21.1 us -> 0.02 us  [per_device(): lax.psum_scatter(jnp.dot(attention, out_weight, preferred_element_type=jn...]
  transfers between devices with their start and end apart: 30 -> 32, of which waited for: 15 -> 15; matrix products, arithmetic and copies ran while one was open for 5% -> 9% of each run, Pallas kernels for 0% -> 0%
where the time goes in v1:
time: 855 us; the launch traced here: 853 us
  waiting for transfers between devices  596 us (70%)
  starting transfers between devices  132 us (15%)
  local copies, waits for them, and re-layouts  72.3 us (8%)
  matrix products  33.7 us (4%)
  between operations  14 us (2%)
    ppermute x2, waiting for transfers between devices, collect(): earlier.append(lax.ppermute(earlier[-1], axis, up))  248 us
    all_gather x1, waiting for transfers between devices, per_device(): lax.all_gather(down_weight, 'head', axis=1, tiled=True)  198 us
    ppermute x1, waiting for transfers between devices, collect(): later.append(lax.ppermute(later[-1], axis, down))  118 us
    ppermute x21, starting transfers between devices, passed_along(): return lax.ppermute(value, axis, pairs)  62.7 us
    ppermute x2, starting transfers between devices, collect(): earlier.append(lax.ppermute(earlier[-1], axis, up))  46.3 us
    unnamed x30, local copies, waits for them, and re-layouts  27.3 us
  transfers between devices with their start and end apart: 32, of which 15 were waited for; matrix products, arithmetic and copies ran while one was open for 9% of the time, Pallas kernels for 0%

profile of v1, /device:TPU:0, one launch (start us, length us, event | category | flops | bytes accessed | tf_op | source)
XLA Modules:
  0.0 853.0 jit_solution(9249674297315324783)
XLA Ops:
  9.2 6.3 all-to-all-start
  36.5 88.7 %while.23 = (s32[]{:T(128)}, bf16[128,576]{1,0:T(8,128)(2,1)}, bf16[128,576]{1,0:T(8,128)(2,1)}, s32[128]{0:T(128)S(1)}, bf16[1024,576]{1,0:T(8,128)(2,1)}, /*in...) while((s32[]{:T(128)}, bf16[128,576]{1,0:T(8,128)(2,1)}, ...), condition=%wide.region_1.2_spmd, body=%wide.region_0.1_spmd.sunk | while | flops 7 | bytes 2396467 | solution.py:118
  37.8 4.1 collective-permute-start.1
  50.9 4.2 collective-permute-start.1
  60.7 4.3 collective-permute-start
  65.0 4.2 collective-permute-start.1
  77.6 4.2 collective-permute-start.1
  90.2 4.2 collective-permute-start.1
  102.8 4.2 collective-permute-start.1
  115.5 4.2 collective-permute-start.1
  132.0 5.3 fusion.48
  144.9 124.4 %collective-permute-done.3 = bf16[2304,720]{0,1:T(8,128)(2,1)} collective-permute-done((bf16[2304,720]{0,1:T(8,128)(2,1)}, bf16[2304,720]{0,1:T(8,128)(2,1)}, u32[]{:S(2)}, u32[]{:S(2)}) %collective-permute-start.3) | collective-permute-done | bytes 3317792 | tf_op jit(solution)/shard_map/ppermute | solution.py:21
  269.2 44.3 %collective-permute-start.4 = (bf16[2304,720]{0,1:T(8,128)(2,1)}, bf16[2304,720]{0,1:T(8,128)(2,1)}, u32[]{:S(2)}, u32[]{:S(2)}) collective-permute-start(bf16[2304,720]{0,1:T(8,128)(2,1)} %collective-permute-done.3), channel_id=1, source_target_pairs={{0,1},{1,2},{2,3},{3,0},{4,5},{5,6},{6,7},{7,4},{8,9},{9,10},{10,1... | collective-permute-start | bytes 9953288 | tf_op jit(solution)/shard_map/ppermute | solution.py:21
  316.8 6.0 all-to-all-start.3
  324.6 8.6 %all-to-all-done.3 = bf16[8,9,2304]{2,1,0:T(8,128)(2,1)S(1)} async-done(((bf16[8,9,2304]{2,1,0:T(8,128)(2,1)}), bf16[8,9,2304]{2,1,0:T(8,128)(2,1)S(1)}, u32[]{:S(2)}, u32[]{:S(2)}) %all-to-all-start.3) | async-done | bytes 331808 | tf_op jit(solution)/shard_map/all_to_all | solution.py:177
  333.4 123.7 %collective-permute-done.4 = bf16[2304,720]{0,1:T(8,128)(2,1)} collective-permute-done((bf16[2304,720]{0,1:T(8,128)(2,1)}, bf16[2304,720]{0,1:T(8,128)(2,1)}, u32[]{:S(2)}, u32[]{:S(2)}) %collective-permute-start.4) | collective-permute-done | bytes 3317792 | tf_op jit(solution)/shard_map/ppermute | solution.py:21
  466.9 117.8 %collective-permute-done.5 = bf16[2304,720]{0,1:T(8,128)(2,1)} collective-permute-done((bf16[2304,720]{0,1:T(8,128)(2,1)}, bf16[2304,720]{0,1:T(8,128)(2,1)}, u32[]{:S(2)}, u32[]{:S(2)}) %collective-permute-start.5) | collective-permute-done | bytes 3317792 | tf_op jit(solution)/shard_map/ppermute | solution.py:23
  588.7 4.4 constant_dynamic-update-slice_fusion.5
  593.1 4.2 constant_dynamic-update-slice_fusion.4
  603.1 9.0 %fusion.53 = f32[72,2880]{1,0:T(8,128)S(1)} fusion(bf16[72,2304]{1,0:T(8,128)(2,1)S(1)} %reshape.164, bf16[2304,2880]{0,1:T(8,128)(2,1)} %all-gather.3.cloned.1.call-done), kind=kOutput, calls=%fused_computation.70 | convolution fusion | flops 955514880 | bytes 14432256 | tf_op jit(solution)/shard_map/dot_general | solution.py:181
  612.1 197.9 %all-gather.5.cloned.1.call-done = bf16[2304,2880]{0,1:T(8,128)(2,1)} async-done(((bf16[2304,720]{0,1:T(8,128)(2,1)}), bf16[2304,2880]{0,1:T(8,128)(2,1)}) %all-gather.5.cloned.1.call-update) | async-done | bytes 13271056 | tf_op jit(solution)/shard_map/all_gather | solution.py:71
  810.0 14.9 %convolution_convert_fusion.1 = bf16[72,2304]{1,0:T(8,128)(2,1)S(1)} fusion(bf16[2304,2880]{0,1:T(8,128)(2,1)} %all-gather.5.cloned.1.call-done, f32[72,2880]{1,0:T(8,128)S(1)} %fusion.53, bf16[72,2304]{1,0:T(8,128)(2,1)S(1)} %reshape.164, bf16[2304,5760]{0,1:T(8,128)(2,1)} %constant_dynamic-update-slice_fusion.2, s32[]{:T(128)S(6)} %select_n.45), kind=kOutput, calls=%fused_computation.11 | convolution fusion | flops 1912439808 | bytes 28035076 | tf_op jit(solution)/shard_map/dot_general | solution.py:183
  825.9 4.2 all-to-all-start.4
  830.1 10.4 %all-to-all-done.4 = bf16[8,9,2304]{2,1,0:T(8,128)(2,1)} async-done(((bf16[8,9,2304]{2,1,0:T(8,128)(2,1)}), bf16[8,9,2304]{2,1,0:T(8,128)(2,1)}, u32[]{:S(2)}, u32[]{:S(2)}) %all-to-all-start.4) | async-done | bytes 331808 | tf_op jit(solution)/shard_map/all_to_all | solution.py:186
  (161 shorter events, 124.1 us)
Async XLA Ops:
  9.2 12.7 %all-to-all-start = ((bf16[32,4,576]{2,0,1:T(8,128)(2,1)}), bf16[32,4,576]{2,0,1:T(8,128)(2,1)S(1)}, u32[]{:S(2)}, u32[]{:S(2)}) async-start(bf16[32,4,576]{2,0,1:T(8,128)(2,1)} %copy.57), calls=%async_computation | async-start | bytes 327680 | tf_op jit(solution)/shard_map/all_to_all | solution.py:84
  21.9 9.3 %all-to-all-start.1 = ((bf16[32,4,576]{2,0,1:T(8,128)(2,1)}), bf16[32,4,576]{2,0,1:T(8,128)(2,1)S(1)}, u32[]{:S(2)}, u32[]{:S(2)}) async-start(bf16[32,4,576]{2,0,1:T(8,128)(2,1)} %copy.58), calls=%async_computation.1 | async-start | bytes 327680 | tf_op jit(solution)/shard_map/all_to_all | solution.py:91
  31.2 96.4 %all-to-all-start.2 = ((bf16[32,4,576]{2,0,1:T(8,128)(2,1)}), bf16[32,4,576]{2,0,1:T(8,128)(2,1)S(1)}, u32[]{:S(2)}, u32[]{:S(2)}) async-start(bf16[32,4,576]{2,0,1:T(8,128)(2,1)} %copy.61), calls=%async_computation.2 | async-start | bytes 327680 | tf_op jit(solution)/shard_map/all_to_all | solution.py:77
  34.6 279.9 %reduce-scatter.2.cloned.1.call-start = ((), (), s32[]{:S(2)}) async-start(), calls=%async_computation.6 | async-start | bytes 737280 | tf_op jit(solution)/shard_map/reduce_scatter | solution.py:145
  37.8 8.4 collective-permute-start.1
  47.5 10.5 %collective-permute-start = (bf16[128,576]{1,0:T(8,128)(2,1)}, bf16[128,576]{1,0:T(8,128)(2,1)S(1)}, u32[]{:S(2)}, u32[]{:S(2)}) collective-permute-start(bf16[128,576]{1,0:T(8,128)(2,1)} %get-tuple-element.230), channel_id=1, source_target_pairs={{0,4},{4,8},{8,12},{12,16},{16,20},{20,24},{24,28},{1,5},{5,9},{9,... | collective-permute-start | bytes 442376 | tf_op jit(solution)/shard_map/while/body/eval_jaxpr/ppermute | solution.py:31
  50.9 8.4 collective-permute-start.1
  60.7 11.4 %collective-permute-start = (bf16[128,576]{1,0:T(8,128)(2,1)}, bf16[128,576]{1,0:T(8,128)(2,1)S(1)}, u32[]{:S(2)}, u32[]{:S(2)}) collective-permute-start(bf16[128,576]{1,0:T(8,128)(2,1)} %get-tuple-element.230), channel_id=1, source_target_pairs={{0,4},{4,8},{8,12},{12,16},{16,20},{20,24},{24,28},{1,5},{5,9},{9,... | collective-permute-start | bytes 442376 | tf_op jit(solution)/shard_map/while/body/eval_jaxpr/ppermute | solution.py:31
  65.0 8.4 collective-permute-start.1
  74.7 9.9 %collective-permute-start = (bf16[128,576]{1,0:T(8,128)(2,1)}, bf16[128,576]{1,0:T(8,128)(2,1)S(1)}, u32[]{:S(2)}, u32[]{:S(2)}) collective-permute-start(bf16[128,576]{1,0:T(8,128)(2,1)} %get-tuple-element.230), channel_id=1, source_target_pairs={{0,4},{4,8},{8,12},{12,16},{16,20},{20,24},{24,28},{1,5},{5,9},{9,... | collective-permute-start | bytes 442376 | tf_op jit(solution)/shard_map/while/body/eval_jaxpr/ppermute | solution.py:31
  77.6 8.4 collective-permute-start.1
  87.4 9.9 %collective-permute-start = (bf16[128,576]{1,0:T(8,128)(2,1)}, bf16[128,576]{1,0:T(8,128)(2,1)S(1)}, u32[]{:S(2)}, u32[]{:S(2)}) collective-permute-start(bf16[128,576]{1,0:T(8,128)(2,1)} %get-tuple-element.230), channel_id=1, source_target_pairs={{0,4},{4,8},{8,12},{12,16},{16,20},{20,24},{24,28},{1,5},{5,9},{9,... | collective-permute-start | bytes 442376 | tf_op jit(solution)/shard_map/while/body/eval_jaxpr/ppermute | solution.py:31
  90.2 8.4 collective-permute-start.1
  100.0 9.9 %collective-permute-start = (bf16[128,576]{1,0:T(8,128)(2,1)}, bf16[128,576]{1,0:T(8,128)(2,1)S(1)}, u32[]{:S(2)}, u32[]{:S(2)}) collective-permute-start(bf16[128,576]{1,0:T(8,128)(2,1)} %get-tuple-element.230), channel_id=1, source_target_pairs={{0,4},{4,8},{8,12},{12,16},{16,20},{20,24},{24,28},{1,5},{5,9},{9,... | collective-permute-start | bytes 442376 | tf_op jit(solution)/shard_map/while/body/eval_jaxpr/ppermute | solution.py:31
  102.8 8.4 collective-permute-start.1
  112.6 9.9 %collective-permute-start = (bf16[128,576]{1,0:T(8,128)(2,1)}, bf16[128,576]{1,0:T(8,128)(2,1)S(1)}, u32[]{:S(2)}, u32[]{:S(2)}) collective-permute-start(bf16[128,576]{1,0:T(8,128)(2,1)} %get-tuple-element.230), channel_id=1, source_target_pairs={{0,4},{4,8},{8,12},{12,16},{16,20},{20,24},{24,28},{1,5},{5,9},{9,... | collective-permute-start | bytes 442376 | tf_op jit(solution)/shard_map/while/body/eval_jaxpr/ppermute | solution.py:31
  115.5 8.4 collective-permute-start.1
  141.4 461.7 %all-gather.3.cloned.1.call-start = ((), (), s32[]{:S(2)}) async-start(), calls=%async_computation.7 | async-start | bytes 16588800 | tf_op jit(solution)/shard_map/all_gather | solution.py:70
  142.2 667.8 %all-gather.5.cloned.1.call-start = ((), (), s32[]{:S(2)}) async-start(), calls=%async_computation.8 | async-start | bytes 16588800 | tf_op jit(solution)/shard_map/all_gather | solution.py:71
  142.9 126.3 %collective-permute-start.3 = (bf16[2304,720]{0,1:T(8,128)(2,1)}, bf16[2304,720]{0,1:T(8,128)(2,1)}, u32[]{:S(2)}, u32[]{:S(2)}) collective-permute-start(bf16[2304,720]{0,1:T(8,128)(2,1)} %param.22), channel_id=1, source_target_pairs={{0,1},{1,2},{2,3},{3,0},{4,5},{5,6},{6,7},{7,4},{8,9},{9,10},{10,1... | collective-permute-start | bytes 9953288 | tf_op jit(solution)/shard_map/ppermute | solution.py:21
  269.2 187.9 %collective-permute-start.4 = (bf16[2304,720]{0,1:T(8,128)(2,1)}, bf16[2304,720]{0,1:T(8,128)(2,1)}, u32[]{:S(2)}, u32[]{:S(2)}) collective-permute-start(bf16[2304,720]{0,1:T(8,128)(2,1)} %collective-permute-done.3), channel_id=1, source_target_pairs={{0,1},{1,2},{2,3},{3,0},{4,5},{5,6},{6,7},{7,4},{8,9},{9,10},{10,1... | collective-permute-start | bytes 9953288 | tf_op jit(solution)/shard_map/ppermute | solution.py:21
  313.5 271.2 %collective-permute-start.5 = (bf16[2304,720]{0,1:T(8,128)(2,1)}, bf16[2304,720]{0,1:T(8,128)(2,1)}, u32[]{:S(2)}, u32[]{:S(2)}) collective-permute-start(bf16[2304,720]{0,1:T(8,128)(2,1)} %param.22), channel_id=1, source_target_pairs={{0,3},{1,0},{2,1},{3,2},{4,7},{5,4},{6,5},{7,6},{8,11},{9,8},{10,9... | collective-permute-start | bytes 9953288 | tf_op jit(solution)/shard_map/ppermute | solution.py:23
  316.8 16.4 %all-to-all-start.3 = ((bf16[8,9,2304]{2,1,0:T(8,128)(2,1)}), bf16[8,9,2304]{2,1,0:T(8,128)(2,1)S(1)}, u32[]{:S(2)}, u32[]{:S(2)}) async-start(bf16[8,9,2304]{2,1,0:T(8,128)(2,1)} %reshape_broadcast_in_dim_reshape.3), calls=%async_computation.4 | async-start | bytes 1179648 | tf_op jit(solution)/shard_map/all_to_all | solution.py:177
  825.9 14.7 %all-to-all-start.4 = ((bf16[8,9,2304]{2,1,0:T(8,128)(2,1)}), bf16[8,9,2304]{2,1,0:T(8,128)(2,1)}, u32[]{:S(2)}, u32[]{:S(2)}) async-start(bf16[8,9,2304]{2,1,0:T(8,128)(2,1)} %reshape.165), calls=%async_computation.5 | async-start | bytes 1179648 | tf_op jit(solution)/shard_map/all_to_all | solution.py:186
  (17 other events, 906.9 us)
Sparse Core Ops, SparseCore 0:
  141.5 31.7 reduce-scatter.1
  174.8 404.1 all-gather.2
  580.6 229.3 all-gather.4
